TPU v7x, 128 devices: a whole 4x4x4 slice. The times are simulated.
128 devices in a mesh: kv: 4 (over x), tok: 32 (over z, y, core).
Axes of the slice: x: 4, y: 4, z: 4, core: 2. Of those that a mesh axis runs over, the one named last changes fastest.
Arguments:
- dec_tokens: bfloat16 [512, 5120], P('tok', 'kv'), may hold values from -60 to 60
- pre_tokens: bfloat16 [8192, 5120], P('tok', 'kv'), may hold values from -60 to 60
- w_query: bfloat16 [5120, 2560], P(None, 'kv'), may hold values from -0.078125 to 0.078125
- w_keyval: bfloat16 [5120, 2, 512], P(None, None, 'kv'), may hold values from -0.078125 to 0.078125
- b_query: float32 [2560], P('kv'), may hold values from -3 to 3
- b_keyval: float32 [2, 512], P(None, 'kv'), may hold values from -3 to 3
- dec_pool: bfloat16 [2, 393216, 512], P(None, 'tok', 'kv'), may hold values from -72 to 72
- owner_slots: int32 [512], P('tok'), may hold values from 0 to 511, each once
- dec_lengths: int32 [512], P('tok'), may hold values from 1 to 4096, as said below
- pre_cache: bfloat16 [2, 32768, 512], P(None, 'tok', 'kv'), may hold values from -72 to 72
- pre_offsets: int32 [16], replicated, may hold values from 1536 to 2048
Outputs:
- dec_attn: bfloat16 [512, 2560], P('tok', 'kv')
- pre_attn: bfloat16 [8192, 2560], P('tok', 'kv')
- new_pool: bfloat16 [2, 393216, 512], P(None, 'tok', 'kv')
- pre_keyval: bfloat16 [2, 8192, 512], P(None, 'tok', 'kv')
Inputs may be any that keep to these rules, and one draw needn't show every extreme that they name: `dec_lengths`: in the 16 slots of each owner, one length is 512 or more and the others are below 512, so an owner's lengths plus one each sum to at most 12288.
All inputs are finite; a program needn't handle non-finite values.
Results may differ from a plain program's by a relative error of at most 0.0065.
The roundings to bfloat16 on the way count: a program that leaves them out, or rounds other values in their place, can miss the bound.
Values may be sent and summed in bfloat16 or wider, within the bound.
No kernel may reach another device: no remote copies, remote signals or barrier semaphores. Data moves between devices by JAX's collectives and lax.ppermute only.
A program may use at most 128 MiB of HBM per device.

v0:
```python
import jax
import jax.numpy as jnp
from jax import lax
from jax.sharding import PartitionSpec as P

HD = 128
THETA = 1000000.0


def swapped(value, axis, distance):
    return lax.ppermute(value, axis, [(i, i ^ 1 << distance) for i in range(lax.axis_size(axis))])


def rotate(values, positions):
    halfway = values.shape[-1] // 2
    spread = jnp.arange(halfway, dtype=jnp.float32) * (2.0 / values.shape[-1])
    rates = jnp.power(jnp.float32(THETA), -spread)
    angles = positions.astype(jnp.float32)[:, None] * rates[None, :]
    cosine = jnp.cos(angles)[:, None, :]
    sine = jnp.sin(angles)[:, None, :]
    former = values[..., :halfway]
    latter = values[..., halfway:]
    return jnp.concatenate(
        [former * cosine - latter * sine, latter * cosine + former * sine], axis=-1
    )


def head_scores(queries, key_rows, allowed):
    amount = queries.shape[0]
    q_heads = queries.shape[1] // HD
    shaped = queries.reshape(amount, q_heads, HD)
    product = jnp.einsum("ngd,md->ngm", shaped, key_rows, preferred_element_type=jnp.float32)
    scores = product * HD ** (-0.5)
    return jnp.where(allowed[:, None, :], scores, -jnp.inf)


def head_mix(scores, peaks, value_rows):
    powers = jnp.exp(scores - peaks[..., None])
    totals = jnp.sum(powers, axis=-1)
    weights = powers.astype(jnp.bfloat16)
    product = jnp.einsum("ngm,md->ngd", weights, value_rows, preferred_element_type=jnp.float32)
    return (totals, product)


def serve_owner(queries, keyval, lengths, cache_pool):
    amount = queries.shape[0]
    q_heads = queries.shape[1] // HD
    kv_heads = cache_pool.shape[2] // HD
    finish = jnp.cumsum(lengths + 1)
    starts = finish - lengths - 1
    turned = rotate(queries.astype(jnp.float32).reshape(amount, q_heads, HD), lengths)
    turned = turned.astype(jnp.bfloat16).reshape(amount, q_heads * HD)
    new_keys = rotate(keyval[:, 0].astype(jnp.float32).reshape(amount, kv_heads, HD), lengths)
    new_keys = new_keys.astype(jnp.bfloat16).reshape(amount, kv_heads * HD)
    appended = jnp.stack([new_keys, keyval[:, 1]], axis=0)
    cache_pool = cache_pool.at[:, starts + lengths].set(appended)
    spots = jnp.arange(cache_pool.shape[1], dtype=jnp.int32)
    allowed = (spots[None, :] >= starts[:, None]) & (spots[None, :] <= (starts + lengths)[:, None])
    scores = head_scores(turned, cache_pool[0], allowed)
    totals, mixed = head_mix(scores, jnp.max(scores, axis=-1), cache_pool[1])
    result = (mixed / totals[..., None]).astype(jnp.bfloat16).reshape(amount, q_heads * HD)
    return (result, cache_pool)


def tree_gather(value):
    place = lax.axis_index("tok")
    buffer = value
    for stride, count in ((1, 2), (2, 4), (8, 4)):
        parts = [buffer]
        for shift in range(1, count):
            pairs = []
            for i in range(32):
                digit = i // stride % count
                target = i + ((digit + shift) % count - digit) * stride
                pairs.append((i, target))
            parts.append(lax.ppermute(buffer, "tok", pairs))
        buffer = jnp.concatenate(parts, axis=0)
    return buffer


def tree_row(place, source, rows):
    core = place % 2 ^ source % 2
    y = (place // 2 % 4 - source // 2 % 4) % 4
    z = (place // 8 - source // 8) % 4
    return ((z * 4 + y) * 2 + core) * rows


def project(rows, w_query, kv_weight, b_query, kv_bias):
    cols = lax.all_gather(rows, "kv", axis=1, tiled=True)
    query = jnp.dot(cols, w_query, preferred_element_type=jnp.float32) + b_query
    keyval = jnp.dot(cols, kv_weight, preferred_element_type=jnp.float32) + kv_bias
    return (query, keyval)


def body(
    dec_tokens,
    pre_tokens,
    w_query,
    w_keyval,
    b_query,
    b_keyval,
    dec_pool,
    owner_slots,
    dec_lengths,
    pre_cache,
    pre_offsets,
):
    dec_count = dec_tokens.shape[0]
    pre_count = pre_tokens.shape[0]
    q_width = w_query.shape[1]
    kv_width = w_keyval.shape[2]
    kv_weight = w_keyval.reshape(w_keyval.shape[0], 2 * kv_width)
    kv_bias = b_keyval.reshape(2 * kv_width)
    dec_q, dec_kv = project(dec_tokens, w_query, kv_weight, b_query, kv_bias)
    tok_place = lax.axis_index("tok")
    ids = jnp.stack([owner_slots // dec_count, owner_slots % dec_count], axis=1).astype(
        jnp.bfloat16
    )
    used = q_width + 2 * kv_width + 2
    pad = jnp.zeros((dec_count, -(-used // 128) * 128 - used), jnp.bfloat16)
    sent = jnp.concatenate(
        [dec_q.astype(jnp.bfloat16), dec_kv.astype(jnp.bfloat16), ids, pad], axis=1
    )
    got = tree_gather(sent)
    rows = tree_row(tok_place, owner_slots // dec_count, dec_count) + owner_slots % dec_count
    chosen = jnp.take(got, rows, axis=0)
    dec_query = chosen[:, :q_width]
    dec_keyval = chosen[:, q_width : q_width + 2 * kv_width].reshape(dec_count, 2, kv_width)
    served, new_pool = serve_owner(dec_query, dec_keyval, dec_lengths, dec_pool)
    back = tree_gather(served)
    got_ids = got[:, q_width + 2 * kv_width : used].astype(jnp.int32)
    requests = got_ids[:, 0] * dec_count + got_ids[:, 1]
    wanted = tok_place * dec_count + jnp.arange(dec_count, dtype=jnp.int32)
    where = jnp.argmax(requests[None, :] == wanted[:, None], axis=1)
    dec_attn = jnp.take(back, where, axis=0)
    all_query, all_keyval = project(pre_tokens, w_query, kv_weight, b_query, kv_bias)
    half_id = tok_place % 2
    offset = pre_offsets[tok_place // 2]
    local_pos = jnp.arange(pre_count, dtype=jnp.int32)
    positions = offset + half_id * pre_count + local_pos
    q_heads = q_width // HD
    kv_heads = kv_width // HD
    turned = rotate(all_query.reshape(pre_count, q_heads, HD), positions)
    turned = turned.astype(jnp.bfloat16).reshape(pre_count, q_width)
    pre_kv = all_keyval.reshape(pre_count, 2, kv_width)
    new_keys = rotate(pre_kv[:, 0].reshape(pre_count, kv_heads, HD), positions)
    new_keys = new_keys.astype(jnp.bfloat16).reshape(pre_count, kv_width)
    appended = jnp.stack([new_keys, pre_kv[:, 1].astype(jnp.bfloat16)], axis=0)
    shard = pre_cache.shape[1]
    other_cache, other_new = swapped((pre_cache, appended), "tok", 0)
    is_lower = half_id == 0
    history = jnp.where(
        is_lower,
        jnp.concatenate([pre_cache, other_cache], axis=1),
        jnp.concatenate([other_cache, pre_cache], axis=1),
    )
    block_rows = jnp.where(
        is_lower,
        jnp.concatenate([appended, other_new], axis=1),
        jnp.concatenate([other_new, appended], axis=1),
    )
    key_rows = jnp.concatenate([history, block_rows], axis=1)
    key_slots = jnp.arange(key_rows.shape[1], dtype=jnp.int32)
    key_pos = jnp.where(key_slots < 2 * shard, key_slots, offset + key_slots - 2 * shard)
    usable = (key_slots < offset) | (key_slots >= 2 * shard)
    allowed = usable[None, :] & (key_pos[None, :] <= positions[:, None])
    scores = head_scores(turned, key_rows[0], allowed)
    totals, mixed = head_mix(scores, jnp.max(scores, axis=-1), key_rows[1])
    pre_attn = (mixed / totals[..., None]).astype(jnp.bfloat16).reshape(pre_count, q_width)
    return (dec_attn, pre_attn, new_pool, appended)


def solution(mesh):
    in_specs = (
        P("tok", "kv"),
        P("tok", "kv"),
        P(None, "kv"),
        P(None, None, "kv"),
        P("kv"),
        P(None, "kv"),
        P(None, "tok", "kv"),
        P("tok"),
        P("tok"),
        P(None, "tok", "kv"),
        P(),
    )
    out_specs = (P("tok", "kv"), P("tok", "kv"), P(None, "tok", "kv"), P(None, "tok", "kv"))
    return jax.shard_map(body, mesh=mesh, in_specs=in_specs, out_specs=out_specs, check_vma=False)
```

profile of v0, /device:TPU:1, one launch (start us, length us, event | category | flops | bytes accessed | tf_op | source)
XLA Modules:
  0.0 154.6 jit_solution(9778527914307117133)
XLA Ops:
  7.3 6.7 %copy.126 = bf16[2,12288,128]{2,1,0:T(8,128)(2,1)} copy(bf16[2,12288,128]{2,1,0:T(8,128)(2,1)} %param.17) | data formatting | bytes 12582912
  16.3 9.8 %all_gather.6 = bf16[16,5120]{1,0:T(8,128)(2,1)S(1)} all-gather(bf16[16,1280]{1,0:T(8,128)(2,1)S(1)} %copy-done.5), channel_id=1, replica_groups=mesh['kv'=4,'tok'=32] {'kv'}, dimensions={1}, use_global_device_ids=true | all-gather | bytes 204800 | tf_op jit(solution)/shard_map/all_gather | solution.py:89
  26.6 4.2 %fusion.21 = bf16[16,640]{1,0:T(8,128)(2,1)S(1)} fusion(bf16[16,5120]{1,0:T(8,128)(2,1)S(1)} %all_gather.6, bf16[5120,640]{1,0:T(8,128)(2,1)} %param.13, f32[640]{0:T(1024)S(1)} %copy-done.8), kind=kOutput, calls=%fused_computation.31 | convolution fusion | flops 104878080 | bytes 6740480 | tf_op jit(solution)/shard_map/dot_general | solution.py:90
  30.9 2.3 %collective-permute-start = (bf16[16,1024]{1,0:T(8,128)(2,1)S(1)}, bf16[16,1024]{1,0:T(8,128)(2,1)S(1)}, u32[]{:S(2)}, u32[]{:S(2)}) collective-permute-start(bf16[16,1024]{1,0:T(8,128)(2,1)S(1)} %concatenate.83), channel_id=1, source_target_pairs={{0,1},{1,0},{2,3},{3,2},{4,5},{5,4},{6,7},{7,6},{8,9},{9,8},{10,11... | collective-permute-start | bytes 98312 | tf_op jit(solution)/shard_map/ppermute | solution.py:76
  42.5 2.6 %collective-permute-start.2 = (bf16[32,1024]{1,0:T(8,128)(2,1)S(1)}, bf16[32,1024]{1,0:T(8,128)(2,1)S(1)}, u32[]{:S(2)}, u32[]{:S(2)}) collective-permute-start(bf16[32,1024]{1,0:T(8,128)(2,1)S(1)} %pad_maximum_fusion.2), channel_id=1, source_target_pairs={{0,4},{1,5},{2,6},{3,7},{4,0},{5,1},{6,2},{7,3},{8,12},{9,13},{10,... | collective-permute-start | bytes 196616 | tf_op jit(solution)/shard_map/ppermute | solution.py:76
  52.4 3.4 %collective-permute-start.5 = (bf16[128,1024]{1,0:T(8,128)(2,1)}, bf16[128,1024]{1,0:T(8,128)(2,1)}, u32[]{:S(2)}, u32[]{:S(2)}) collective-permute-start(bf16[128,1024]{1,0:T(8,128)(2,1)} %get-tuple-element.36), channel_id=1, source_target_pairs={{0,16},{1,17},{2,18},{3,19},{4,20},{5,21},{6,22},{7,23},{8,24},{9,... | collective-permute-start | bytes 786440 | tf_op jit(solution)/shard_map/ppermute | solution.py:76
  57.8 2.1 %collective-permute-done.4 = bf16[128,1024]{1,0:T(8,128)(2,1)} collective-permute-done((bf16[128,1024]{1,0:T(8,128)(2,1)}, bf16[128,1024]{1,0:T(8,128)(2,1)}, u32[]{:S(2)}, u32[]{:S(2)}) %collective-permute-start.4) | collective-permute-done | bytes 262176 | tf_op jit(solution)/shard_map/ppermute | solution.py:76
  59.9 1.7 %constant_dynamic-update-slice_fusion.7 = bf16[512,1024]{1,0:T(8,128)(2,1)} fusion(bf16[512,1024]{1,0:T(8,128)(2,1)} %get-tuple-element.37, bf16[128,1024]{1,0:T(8,128)(2,1)} %collective-permute-done.4), kind=kLoop, calls=%fused_computation.83 | loop fusion | bytes 524288
  61.5 4.8 %collective-permute-done.5 = bf16[128,1024]{1,0:T(8,128)(2,1)} collective-permute-done((bf16[128,1024]{1,0:T(8,128)(2,1)}, bf16[128,1024]{1,0:T(8,128)(2,1)}, u32[]{:S(2)}, u32[]{:S(2)}) %collective-permute-start.5) | collective-permute-done | bytes 262176 | tf_op jit(solution)/shard_map/ppermute | solution.py:76
  69.7 2.0 %gather_fusion = bf16[16,1024]{1,0:T(8,128)(2,1)S(1)} fusion(bf16[512,1024]{1,0:T(8,128)(2,1)} %constant_dynamic-update-slice_fusion.5, s32[1024]{0:T(1024)S(1)} %pad_clamp_fusion.1), kind=kCustom, calls=%fused_computation | custom fusion | bytes 65600 | tf_op jit(solution)/shard_map/jit(_take)/gather | solution.py:126
  76.8 2.4 %scatter_fusion = bf16[2,12288,128]{2,1,0:T(8,128)(2,1)} fusion(bf16[2,12288,128]{2,1,0:T(8,128)(2,1)} %copy.126, s32[16]{0:T(128)} %get-tuple-element.22, bf16[16,2,128]{2,0,1:T(8,128)(2,1)S(1)} %maximum_bitcast_fusion), kind=kCustom, calls=%fused_computation.2 | custom fusion | bytes 24640 | tf_op jit(solution)/shard_map/scatter | solution.py:56
  80.3 3.5 %fusion.100 = (f32[16,5]{0,1:T(8,128)S(1)}, f32[16,5,12288]{2,0,1:T(8,128)S(1)}) fusion(bf16[2,12288,128]{2,1,0:T(8,128)(2,1)} %scatter_fusion, bf16[16,5,64]{2,0,1:T(8,128)(2,1)S(1)} %get-tuple-element.33, bf16[16,5,64]{2,0,1:T(8,128)(2,1)S(1)} %get-tuple-element.32, pred[16,12288]{1,0:T(8,128)(4,1)S(1)} %fusion.43), kind=kOutput, calls=%fused_computation.192 | convolution fusion | flops 254648240 | bytes 7295296 | tf_op jit(solution)/shard_map/ngd,md->ngm/dot_general | solution.py:32
  85.5 1.8 %collective-permute-start.7 = (bf16[16,640]{1,0:T(8,128)(2,1)S(1)}, bf16[16,640]{1,0:T(8,128)(2,1)S(1)}, u32[]{:S(2)}, u32[]{:S(2)}) collective-permute-start(bf16[16,640]{1,0:T(8,128)(2,1)S(1)} %bitcast.93), channel_id=1, source_target_pairs={{0,1},{1,0},{2,3},{3,2},{4,5},{5,4},{6,7},{7,6},{8,9},{9,8},{10,11... | collective-permute-start | bytes 61448 | tf_op jit(solution)/shard_map/ppermute | solution.py:76
  90.6 2.6 %collective-permute-start.9 = (bf16[32,640]{1,0:T(8,128)(2,1)S(1)}, bf16[32,640]{1,0:T(8,128)(2,1)S(1)}, u32[]{:S(2)}, u32[]{:S(2)}) collective-permute-start(bf16[32,640]{1,0:T(8,128)(2,1)S(1)} %get-tuple-element.54), channel_id=1, source_target_pairs={{0,4},{1,5},{2,6},{3,7},{4,0},{5,1},{6,2},{7,3},{8,12},{9,13},{10,... | collective-permute-start | bytes 122888 | tf_op jit(solution)/shard_map/ppermute | solution.py:76
  97.4 1.7 %collective-permute-start.12 = (bf16[128,640]{1,0:T(8,128)(2,1)S(1)}, bf16[128,640]{1,0:T(8,128)(2,1)S(1)}, u32[]{:S(2)}, u32[]{:S(2)}) collective-permute-start(bf16[128,640]{1,0:T(8,128)(2,1)S(1)} %get-tuple-element.42), channel_id=1, source_target_pairs={{0,16},{1,17},{2,18},{3,19},{4,20},{5,21},{6,22},{7,23},{8,24},{9,... | collective-permute-start | bytes 491528 | tf_op jit(solution)/shard_map/ppermute | solution.py:76
  99.1 1.7 %collective-permute-start.13 = (bf16[128,640]{1,0:T(8,128)(2,1)S(1)}, bf16[128,640]{1,0:T(8,128)(2,1)S(1)}, u32[]{:S(2)}, u32[]{:S(2)}) collective-permute-start(bf16[128,640]{1,0:T(8,128)(2,1)S(1)} %get-tuple-element.42), channel_id=1, source_target_pairs={{0,24},{1,25},{2,26},{3,27},{4,28},{5,29},{6,30},{7,31},{8,0},{9,1... | collective-permute-start | bytes 491528 | tf_op jit(solution)/shard_map/ppermute | solution.py:76
  100.8 2.8 %maximum_select_fusion = bf16[2,2048,128]{2,1,0:T(8,128)(2,1)} fusion(bf16[2,1024,128]{2,1,0:T(8,128)(2,1)} %collective-permute-done.14, bf16[2,1024,128]{2,1,0:T(8,128)(2,1)} %param.20, pred[]{:T(512)S(6)} %eq.32), kind=kLoop, calls=%fused_computation.37 | loop fusion | flops 4718592 | bytes 2097153 | tf_op jit(solution)/shard_map/jit(_where)/select_n | solution.py:152
  106.8 1.8 %gather_fusion.1 = bf16[16,640]{1,0:T(8,128)(2,1)S(1)} fusion(bf16[512,640]{1,0:T(8,128)(2,1)} %constant_dynamic-update-slice_fusion.20, s32[1024]{0:T(1024)S(1)} %pad_clamp_fusion), kind=kCustom, calls=%fused_computation.1 | custom fusion | bytes 41024 | tf_op jit(solution)/shard_map/jit(_take)/gather | solution.py:135
  109.3 2.9 %fusion.18 = f32[256,256]{0,1:T(8,128)S(1)} fusion(bf16[256,5120]{1,0:T(8,128)(2,1)} %all-gather.2.cloned.1.call-done, bf16[640,8,2,128]{3,2,1,0:T(2,128)(2,1)S(1)} %bitcast.86, f32[256]{0:T(256)S(1)} %bitcast.96), kind=kOutput, calls=%fused_computation.29 | convolution fusion | flops 671154176 | bytes 5506048 | tf_op jit(solution)/shard_map/dot_general | solution.py:91
  113.3 3.7 %collective-permute-start.15 = (bf16[2,256,128]{2,1,0:T(8,128)(2,1)S(1)}, bf16[2,256,128]{2,1,0:T(8,128)(2,1)S(1)}, u32[]{:S(2)}, u32[]{:S(2)}) collective-permute-start(bf16[2,256,128]{2,1,0:T(8,128)(2,1)S(1)} %pad_maximum_fusion.1), channel_id=1, source_target_pairs={{0,1},{1,0},{2,3},{3,2},{4,5},{5,4},{6,7},{7,6},{8,9},{9,8},{10,11... | collective-permute-start | bytes 393224 | tf_op jit(solution)/shard_map/ppermute | solution.py:11
  117.0 5.9 %convolution_add_fusion = f32[256,640]{1,0:T(8,128)S(1)} fusion(bf16[256,5120]{1,0:T(8,128)(2,1)} %all-gather.2.cloned.1.call-done, bf16[5120,640]{1,0:T(8,128)(2,1)} %param.13, f32[640]{0:T(1024)S(1)} %copy-done.9), kind=kOutput, calls=%fused_computation.28 | convolution fusion | flops 1677885440 | bytes 9832960 | tf_op jit(solution)/shard_map/dot_general | solution.py:90
  124.2 7.2 %fusion.1 = (f32[256,5]{0,1:T(8,128)S(1)}, f32[256,5,2560]{2,0,1:T(8,128)}) fusion(pred[256,2560]{1,0:T(8,128)(4,1)S(1)} %compare_and_fusion, bf16[2,2048,128]{2,1,0:T(8,128)(2,1)} %maximum_select_fusion, bf16[2,512,128]{2,1,0:T(8,128)(2,1)S(1)} %maximum_select_fusion.1, bf16[256,5,64]{2,0,1:T(8,128)(2,1)S(1)} %get-tuple-element.25, ...), kind=kOutput, calls=%fused_computation.7 | convolution fusion | flops 850656000 | bytes 15406080 | tf_op jit(solution)/shard_map/ngd,md->ngm/dot_general | solution.py:32
  131.4 8.5 %fusion.2 = f32[256,5]{0,1:T(8,128)S(1)} fusion(f32[256,5,2560]{2,0,1:T(8,128)} %get-tuple-element.72, f32[256,5]{0,1:T(8,128)S(1)} %get-tuple-element.71, pred[256,2560]{1,0:T(8,128)(4,1)S(1)} %compare_and_fusion), kind=kLoop, calls=%fused_computation.8 | loop fusion | flops 13105920 | bytes 13772800 | tf_op jit(solution)/shard_map/reduce_sum | solution.py:39
  139.9 7.0 %fusion.40 = bf16[256,5,128]{0,2,1:T(8,128)(2,1)S(1)} fusion(f32[256,5,2560]{2,0,1:T(8,128)} %get-tuple-element.72, f32[256,5]{0,1:T(8,128)S(1)} %get-tuple-element.71, pred[256,2560]{1,0:T(8,128)(4,1)S(1)} %compare_and_fusion, bf16[2,512,128]{2,1,0:T(8,128)(2,1)S(1)} %maximum_select_fusion.1, bf16[2,2048,128]{2,1,0:T(8,128)(2,1)S(1)} %copy-done.1, ...), kind=kOutput, calls=%fused_computation.39 | convolution fusion | flops 853606400 | bytes 15411200 | tf_op jit(solution)/shard_map/ngm,md->ngd/dot_general | solution.py:41
  (142 shorter events, 46.4 us)
Async XLA Ops:
  7.2 9.1 %copy-start.5 = (bf16[16,1280]{1,0:T(8,128)(2,1)S(1)}, bf16[16,1280]{1,0:T(8,128)(2,1)}, u32[]{:S(2)}) copy-start(bf16[16,1280]{1,0:T(8,128)(2,1)} %param.11) | copy-start | bytes 122884
  7.2 18.9 %copy-start.12 = (f32[2,128]{1,0:T(2,128)S(1)}, f32[2,128]{1,0:T(2,128)}, u32[]{:S(2)}) copy-start(f32[2,128]{1,0:T(2,128)} %param.16) | copy-start | bytes 3076
  7.2 18.9 %copy-start = (bf16[5120,2,128]{2,1,0:T(2,128)(2,1)S(1)}, bf16[5120,2,128]{2,1,0:T(2,128)(2,1)}, u32[]{:S(2)}) copy-start(bf16[5120,2,128]{2,1,0:T(2,128)(2,1)} %param.14) | copy-start | bytes 7864324
  7.2 19.4 %copy-start.8 = (f32[640]{0:T(1024)S(1)}, f32[640]{0:T(1024)}, u32[]{:S(2)}) copy-start(f32[640]{0:T(1024)} %param.15) | copy-start | bytes 7684
  7.2 102.1 %all-gather.2.cloned.1.call-start = ((), (), s32[]{:S(2)}) async-start(), calls=%async_computation | async-start | bytes 3276800 | tf_op jit(solution)/shard_map/all_gather | solution.py:89
  14.0 86.8 %collective-permute-start.14 = (bf16[2,1024,128]{2,1,0:T(8,128)(2,1)}, bf16[2,1024,128]{2,1,0:T(8,128)(2,1)}, u32[]{:S(2)}, u32[]{:S(2)}) collective-permute-start(bf16[2,1024,128]{2,1,0:T(8,128)(2,1)} %param.20), channel_id=1, source_target_pairs={{0,1},{1,0},{2,3},{3,2},{4,5},{5,4},{6,7},{7,6},{8,9},{9,8},{10,11... | collective-permute-start | bytes 1572872 | tf_op jit(solution)/shard_map/ppermute | solution.py:11
  26.6 9.9 %copy-start.14 = (s32[16]{0:T(128)S(1)}, s32[16]{0:T(128)}, u32[]{:S(2)}) copy-start(s32[16]{0:T(128)} %param.19) | copy-start | bytes 196
  30.9 10.2 %collective-permute-start = (bf16[16,1024]{1,0:T(8,128)(2,1)S(1)}, bf16[16,1024]{1,0:T(8,128)(2,1)S(1)}, u32[]{:S(2)}, u32[]{:S(2)}) collective-permute-start(bf16[16,1024]{1,0:T(8,128)(2,1)S(1)} %concatenate.83), channel_id=1, source_target_pairs={{0,1},{1,0},{2,3},{3,2},{4,5},{5,4},{6,7},{7,6},{8,9},{9,8},{10,11... | collective-permute-start | bytes 98312 | tf_op jit(solution)/shard_map/ppermute | solution.py:76
  41.2 5.7 %collective-permute-start.1 = (bf16[32,1024]{1,0:T(8,128)(2,1)S(1)}, bf16[32,1024]{1,0:T(8,128)(2,1)S(1)}, u32[]{:S(2)}, u32[]{:S(2)}) collective-permute-start(bf16[32,1024]{1,0:T(8,128)(2,1)S(1)} %pad_maximum_fusion.2), channel_id=1, source_target_pairs={{0,2},{1,3},{2,4},{3,5},{4,6},{5,7},{6,0},{7,1},{8,10},{9,11},{10,... | collective-permute-start | bytes 196616 | tf_op jit(solution)/shard_map/ppermute | solution.py:76
  42.5 6.2 %collective-permute-start.2 = (bf16[32,1024]{1,0:T(8,128)(2,1)S(1)}, bf16[32,1024]{1,0:T(8,128)(2,1)S(1)}, u32[]{:S(2)}, u32[]{:S(2)}) collective-permute-start(bf16[32,1024]{1,0:T(8,128)(2,1)S(1)} %pad_maximum_fusion.2), channel_id=1, source_target_pairs={{0,4},{1,5},{2,6},{3,7},{4,0},{5,1},{6,2},{7,3},{8,12},{9,13},{10,... | collective-permute-start | bytes 196616 | tf_op jit(solution)/shard_map/ppermute | solution.py:76
  45.1 4.2 %collective-permute-start.3 = (bf16[32,1024]{1,0:T(8,128)(2,1)S(1)}, bf16[32,1024]{1,0:T(8,128)(2,1)S(1)}, u32[]{:S(2)}, u32[]{:S(2)}) collective-permute-start(bf16[32,1024]{1,0:T(8,128)(2,1)S(1)} %pad_maximum_fusion.2), channel_id=1, source_target_pairs={{0,6},{1,7},{2,0},{3,1},{4,2},{5,3},{6,4},{7,5},{8,14},{9,15},{10,... | collective-permute-start | bytes 196616 | tf_op jit(solution)/shard_map/ppermute | solution.py:76
  50.0 9.9 %collective-permute-start.4 = (bf16[128,1024]{1,0:T(8,128)(2,1)}, bf16[128,1024]{1,0:T(8,128)(2,1)}, u32[]{:S(2)}, u32[]{:S(2)}) collective-permute-start(bf16[128,1024]{1,0:T(8,128)(2,1)} %get-tuple-element.36), channel_id=1, source_target_pairs={{0,8},{1,9},{2,10},{3,11},{4,12},{5,13},{6,14},{7,15},{8,16},{9,17... | collective-permute-start | bytes 786440 | tf_op jit(solution)/shard_map/ppermute | solution.py:76
  52.4 14.0 %collective-permute-start.5 = (bf16[128,1024]{1,0:T(8,128)(2,1)}, bf16[128,1024]{1,0:T(8,128)(2,1)}, u32[]{:S(2)}, u32[]{:S(2)}) collective-permute-start(bf16[128,1024]{1,0:T(8,128)(2,1)} %get-tuple-element.36), channel_id=1, source_target_pairs={{0,16},{1,17},{2,18},{3,19},{4,20},{5,21},{6,22},{7,23},{8,24},{9,... | collective-permute-start | bytes 786440 | tf_op jit(solution)/shard_map/ppermute | solution.py:76
  56.5 11.6 %collective-permute-start.6 = (bf16[128,1024]{1,0:T(8,128)(2,1)}, bf16[128,1024]{1,0:T(8,128)(2,1)}, u32[]{:S(2)}, u32[]{:S(2)}) collective-permute-start(bf16[128,1024]{1,0:T(8,128)(2,1)} %get-tuple-element.36), channel_id=1, source_target_pairs={{0,24},{1,25},{2,26},{3,27},{4,28},{5,29},{6,30},{7,31},{8,0},{9,1... | collective-permute-start | bytes 786440 | tf_op jit(solution)/shard_map/ppermute | solution.py:76
  85.5 23.8 %copy-start.13 = (f32[2,128]{1,0:T(2,128)S(1)}, f32[2,128]{1,0:T(2,128)}, u32[]{:S(2)}) copy-start(f32[2,128]{1,0:T(2,128)} %param.16) | copy-start | bytes 3076
  85.5 4.3 %collective-permute-start.7 = (bf16[16,640]{1,0:T(8,128)(2,1)S(1)}, bf16[16,640]{1,0:T(8,128)(2,1)S(1)}, u32[]{:S(2)}, u32[]{:S(2)}) collective-permute-start(bf16[16,640]{1,0:T(8,128)(2,1)S(1)} %bitcast.93), channel_id=1, source_target_pairs={{0,1},{1,0},{2,3},{3,2},{4,5},{5,4},{6,7},{7,6},{8,9},{9,8},{10,11... | collective-permute-start | bytes 61448 | tf_op jit(solution)/shard_map/ppermute | solution.py:76
  90.4 4.1 %collective-permute-start.8 = (bf16[32,640]{1,0:T(8,128)(2,1)S(1)}, bf16[32,640]{1,0:T(8,128)(2,1)S(1)}, u32[]{:S(2)}, u32[]{:S(2)}) collective-permute-start(bf16[32,640]{1,0:T(8,128)(2,1)S(1)} %get-tuple-element.54), channel_id=1, source_target_pairs={{0,2},{1,3},{2,4},{3,5},{4,6},{5,7},{6,0},{7,1},{8,10},{9,11},{10,... | collective-permute-start | bytes 122888 | tf_op jit(solution)/shard_map/ppermute | solution.py:76
  90.6 4.8 %collective-permute-start.9 = (bf16[32,640]{1,0:T(8,128)(2,1)S(1)}, bf16[32,640]{1,0:T(8,128)(2,1)S(1)}, u32[]{:S(2)}, u32[]{:S(2)}) collective-permute-start(bf16[32,640]{1,0:T(8,128)(2,1)S(1)} %get-tuple-element.54), channel_id=1, source_target_pairs={{0,4},{1,5},{2,6},{3,7},{4,0},{5,1},{6,2},{7,3},{8,12},{9,13},{10,... | collective-permute-start | bytes 122888 | tf_op jit(solution)/shard_map/ppermute | solution.py:76
  93.2 3.1 %collective-permute-start.10 = (bf16[32,640]{1,0:T(8,128)(2,1)S(1)}, bf16[32,640]{1,0:T(8,128)(2,1)S(1)}, u32[]{:S(2)}, u32[]{:S(2)}) collective-permute-start(bf16[32,640]{1,0:T(8,128)(2,1)S(1)} %get-tuple-element.54), channel_id=1, source_target_pairs={{0,6},{1,7},{2,0},{3,1},{4,2},{5,3},{6,4},{7,5},{8,14},{9,15},{10,... | collective-permute-start | bytes 122888 | tf_op jit(solution)/shard_map/ppermute | solution.py:76
  96.9 6.8 %collective-permute-start.11 = (bf16[128,640]{1,0:T(8,128)(2,1)S(1)}, bf16[128,640]{1,0:T(8,128)(2,1)S(1)}, u32[]{:S(2)}, u32[]{:S(2)}) collective-permute-start(bf16[128,640]{1,0:T(8,128)(2,1)S(1)} %get-tuple-element.42), channel_id=1, source_target_pairs={{0,8},{1,9},{2,10},{3,11},{4,12},{5,13},{6,14},{7,15},{8,16},{9,17... | collective-permute-start | bytes 491528 | tf_op jit(solution)/shard_map/ppermute | solution.py:76
  97.4 7.7 %collective-permute-start.12 = (bf16[128,640]{1,0:T(8,128)(2,1)S(1)}, bf16[128,640]{1,0:T(8,128)(2,1)S(1)}, u32[]{:S(2)}, u32[]{:S(2)}) collective-permute-start(bf16[128,640]{1,0:T(8,128)(2,1)S(1)} %get-tuple-element.42), channel_id=1, source_target_pairs={{0,16},{1,17},{2,18},{3,19},{4,20},{5,21},{6,22},{7,23},{8,24},{9,... | collective-permute-start | bytes 491528 | tf_op jit(solution)/shard_map/ppermute | solution.py:76
  99.1 7.1 %collective-permute-start.13 = (bf16[128,640]{1,0:T(8,128)(2,1)S(1)}, bf16[128,640]{1,0:T(8,128)(2,1)S(1)}, u32[]{:S(2)}, u32[]{:S(2)}) collective-permute-start(bf16[128,640]{1,0:T(8,128)(2,1)S(1)} %get-tuple-element.42), channel_id=1, source_target_pairs={{0,24},{1,25},{2,26},{3,27},{4,28},{5,29},{6,30},{7,31},{8,0},{9,1... | collective-permute-start | bytes 491528 | tf_op jit(solution)/shard_map/ppermute | solution.py:76
  113.3 9.6 %copy-start.4 = (bf16[2,256,128]{2,1,0:T(8,128)(2,1)}, bf16[2,256,128]{2,1,0:T(8,128)(2,1)S(1)}, u32[]{:S(2)}) copy-start(bf16[2,256,128]{2,1,0:T(8,128)(2,1)S(1)} %pad_maximum_fusion.1) | copy-start | bytes 393220
  113.3 10.7 %collective-permute-start.15 = (bf16[2,256,128]{2,1,0:T(8,128)(2,1)S(1)}, bf16[2,256,128]{2,1,0:T(8,128)(2,1)S(1)}, u32[]{:S(2)}, u32[]{:S(2)}) collective-permute-start(bf16[2,256,128]{2,1,0:T(8,128)(2,1)S(1)} %pad_maximum_fusion.1), channel_id=1, source_target_pairs={{0,1},{1,0},{2,3},{3,2},{4,5},{5,4},{6,7},{7,6},{8,9},{9,8},{10,11... | collective-permute-start | bytes 393224 | tf_op jit(solution)/shard_map/ppermute | solution.py:11
  (13 other events, 70.6 us)
Sparse Core Ops, SparseCore 0:
  14.1 38.1 all-gather.1
where the time goes:
time: 155 us
  local copies, waits for them, and re-layouts  32.2 us (21%)
  matrix products  32 us (21%)
  starting transfers between devices  27.6 us (18%)
  other arithmetic  27.3 us (18%)
  between operations  15.1 us (10%)
  waiting for transfers between devices  10.5 us (7%)
  blocking collectives  9.84 us (6%)
    ppermute x14, starting transfers between devices, tree_gather(): parts.append(lax.ppermute(buffer, 'tok', pairs))  22.4 us
    unnamed x60, local copies, waits for them, and re-layouts  18.3 us
    dot_general x2, matrix products, head_scores(): jnp.einsum('ngd,md->ngm', shaped, key_rows, preferred_element_type=jnp.fl...  10.7 us
    ppermute x14, waiting for transfers between devices, tree_gather(): parts.append(lax.ppermute(buffer, 'tok', pairs))  10.5 us
    dot_general x2, matrix products, project(): query = jnp.dot(cols, w_query, preferred_element_type=jnp.float32) + b_query  10.1 us
    all_gather x1, blocking collectives, project(): cols = lax.all_gather(rows, 'kv', axis=1, tiled=True)  9.84 us
    reduce_sum x2, other arithmetic, head_mix(): totals = jnp.sum(powers, axis=-1)  9.29 us
    dot_general x2, matrix products, head_mix(): jnp.einsum('ngm,md->ngd', weights, value_rows, preferred_element_type=jnp...  7.83 us
  transfers between devices with their start and end apart: 17, of which 9 were waited for; matrix products, arithmetic and copies ran while one was open for 37% of the time, Pallas kernels for 0%

commit v1 on v0

--- a/solution.py
+++ b/solution.py
@@ -86,7 +86,9 @@
 
 
 def project(rows, w_query, kv_weight, b_query, kv_bias):
-    cols = lax.all_gather(rows, "kv", axis=1, tiled=True)
+    high = jax.lax.axis_size("kv")
+    opened = jnp.concatenate([rows] * high, axis=1)
+    cols = jax.lax.all_to_all(opened, axis_name="kv", split_axis=1, concat_axis=1, tiled=True)
     query = jnp.dot(cols, w_query, preferred_element_type=jnp.float32) + b_query
     keyval = jnp.dot(cols, kv_weight, preferred_element_type=jnp.float32) + kv_bias
     return (query, keyval)

time: 155 us -> 129 us (0.83)
  between operations: 15.1 us -> 1.85 us
  local copies, waits for them, and re-layouts: 32.2 us -> 22.1 us
  blocking collectives: 9.84 us -> 0 us
  waiting for transfers between devices: 10.5 us -> 19.1 us
  starting transfers between devices: 27.6 us -> 35.5 us
  other arithmetic: 27.3 us -> 21 us
  matrix products: 32 us -> 28.8 us
    all_gather x1 -> x0, blocking collectives: 9.84 us -> none  [project(): cols = lax.all_gather(rows, 'kv', axis=1, tiled=True)]
    unnamed x60 -> x55, local copies, waits for them, and re-layouts: 18.3 us -> 9.27 us
    all_to_all x0 -> x2, starting transfers between devices: none -> 8.8 us  [project(): jax.lax.all_to_all(opened, axis_name='kv', split_axis=1, concat_axis=1, t...]
    ppermute x14, waiting for transfers between devices: 10.5 us -> 18.9 us  [tree_gather(): parts.append(lax.ppermute(buffer, 'tok', pairs))]
    all_to_all x0 -> x4, local copies, waits for them, and re-layouts: none -> 7.84 us  [project(): jax.lax.all_to_all(opened, axis_name='kv', split_axis=1, concat_axis=1, t...]
    dot_general x2, matrix products: 10.1 us -> 6.1 us  [project(): query = jnp.dot(cols, w_query, preferred_element_type=jnp.float32) + b_query]
    concatenate x4, local copies, waits for them, and re-layouts: 3.6 us -> 0.06 us  [tree_gather(): buffer = jnp.concatenate(parts, axis=0)]
  transfers between devices with their start and end apart: 17 -> 18, of which waited for: 9 -> 12; matrix products, arithmetic and copies ran while one was open for 37% -> 22% of each run, Pallas kernels for 0% -> 0%
where the time goes in v1:
time: 129 us; the launch traced here: 128 us
  starting transfers between devices  35.5 us (28%)
  matrix products  28.8 us (22%)
  local copies, waits for them, and re-layouts  22.1 us (17%)
  other arithmetic  21 us (16%)
  waiting for transfers between devices  19.1 us (15%)
  between operations  1.85 us (1%)
    ppermute x14, starting transfers between devices, tree_gather(): parts.append(lax.ppermute(buffer, 'tok', pairs))  21.9 us
    ppermute x14, waiting for transfers between devices, tree_gather(): parts.append(lax.ppermute(buffer, 'tok', pairs))  18.9 us
    dot_general x2, matrix products, head_scores(): jnp.einsum('ngd,md->ngm', shaped, key_rows, preferred_element_type=jnp.fl...  10.6 us
    reduce_sum x2, other arithmetic, head_mix(): totals = jnp.sum(powers, axis=-1)  9.29 us
    unnamed x55, local copies, waits for them, and re-layouts  9.27 us
    all_to_all x2, starting transfers between devices, project(): jax.lax.all_to_all(opened, axis_name='kv', split_axis=1, concat_axis=1, t...  8.8 us
    all_to_all x4, local copies, waits for them, and re-layouts, project(): jax.lax.all_to_all(opened, axis_name='kv', split_axis=1, concat_axis=1, t...  7.84 us
    dot_general x2, matrix products, head_mix(): jnp.einsum('ngm,md->ngd', weights, value_rows, preferred_element_type=jnp...  7.83 us
  transfers between devices with their start and end apart: 18, of which 12 were waited for; matrix products, arithmetic and copies ran while one was open for 22% of the time, Pallas kernels for 0%

profile of v1, /device:TPU:1, one launch (start us, length us, event | category | flops | bytes accessed | tf_op | source)
XLA Modules:
  0.0 128.3 jit_solution(14175342797987073880)
XLA Ops:
  0.7 6.5 %copy.178 = bf16[2,12288,128]{2,1,0:T(8,128)(2,1)} copy(bf16[2,12288,128]{2,1,0:T(8,128)(2,1)} %param.17) | data formatting | bytes 12582912
  9.2 4.1 %all-to-all-start = ((bf16[16,4,1280]{2,0,1:T(8,128)(2,1)}), bf16[16,4,1280]{2,0,1:T(8,128)(2,1)S(1)}, u32[]{:S(2)}, u32[]{:S(2)}) async-start(bf16[16,4,1280]{2,0,1:T(8,128)(2,1)} %bitcast.88), calls=%async_computation | async-start | bytes 327680 | tf_op jit(solution)/shard_map/all_to_all | solution.py:91
  16.8 2.6 %copy.97 = bf16[256,4,1280]{2,0,1:T(8,128)(2,1)} copy(bf16[256,4,1280]{0,2,1:T(8,128)(2,1)S(1)} %bitcast.97) | data formatting | bytes 5242880 | tf_op jit(solution)/shard_map/all_to_all | solution.py:91
  22.7 4.7 %all-to-all-start.1 = ((bf16[256,4,1280]{2,0,1:T(8,128)(2,1)}), bf16[256,4,1280]{2,0,1:T(8,128)(2,1)}, u32[]{:S(2)}, u32[]{:S(2)}) async-start(bf16[256,4,1280]{2,0,1:T(8,128)(2,1)} %copy.97), calls=%async_computation.1 | async-start | bytes 5242880 | tf_op jit(solution)/shard_map/all_to_all | solution.py:91
  27.9 3.8 %fusion.21 = bf16[16,640]{1,0:T(8,128)(2,1)S(1)} fusion(bf16[16,5120]{1,0:T(8,128)(2,1)S(1)} %bitcast.102, bf16[5120,640]{1,0:T(8,128)(2,1)} %param.13, f32[640]{0:T(1024)S(1)} %copy-done.8), kind=kOutput, calls=%fused_computation.32 | convolution fusion | flops 104878080 | bytes 6740480 | tf_op jit(solution)/shard_map/dot_general | solution.py:92
  34.5 2.6 %collective-permute-start.2 = (bf16[32,1024]{1,0:T(8,128)(2,1)S(1)}, bf16[32,1024]{1,0:T(8,128)(2,1)S(1)}, u32[]{:S(2)}, u32[]{:S(2)}) collective-permute-start(bf16[32,1024]{1,0:T(8,128)(2,1)S(1)} %pad_maximum_fusion.4), channel_id=1, source_target_pairs={{0,4},{1,5},{2,6},{3,7},{4,0},{5,1},{6,2},{7,3},{8,12},{9,13},{10,... | collective-permute-start | bytes 196616 | tf_op jit(solution)/shard_map/ppermute | solution.py:76
  38.2 1.8 %collective-permute-done.2 = bf16[32,1024]{1,0:T(8,128)(2,1)S(1)} collective-permute-done((bf16[32,1024]{1,0:T(8,128)(2,1)S(1)}, bf16[32,1024]{1,0:T(8,128)(2,1)S(1)}, u32[]{:S(2)}, u32[]{:S(2)}) %collective-permute-start.2) | collective-permute-done | bytes 65568 | tf_op jit(solution)/shard_map/ppermute | solution.py:76
  42.4 3.4 %collective-permute-start.5 = (bf16[128,1024]{1,0:T(8,128)(2,1)S(1)}, bf16[128,1024]{1,0:T(8,128)(2,1)S(1)}, u32[]{:S(2)}, u32[]{:S(2)}) collective-permute-start(bf16[128,1024]{1,0:T(8,128)(2,1)S(1)} %get-tuple-element.44), channel_id=1, source_target_pairs={{0,16},{1,17},{2,18},{3,19},{4,20},{5,21},{6,22},{7,23},{8,24},{9,... | collective-permute-start | bytes 786440 | tf_op jit(solution)/shard_map/ppermute | solution.py:76
  46.6 3.0 %collective-permute-done.4 = bf16[128,1024]{1,0:T(8,128)(2,1)S(1)} collective-permute-done((bf16[128,1024]{1,0:T(8,128)(2,1)S(1)}, bf16[128,1024]{1,0:T(8,128)(2,1)S(1)}, u32[]{:S(2)}, u32[]{:S(2)}) %collective-permute-start.4) | collective-permute-done | bytes 262176 | tf_op jit(solution)/shard_map/ppermute | solution.py:76
  49.6 6.5 %collective-permute-done.5 = bf16[128,1024]{1,0:T(8,128)(2,1)S(1)} collective-permute-done((bf16[128,1024]{1,0:T(8,128)(2,1)S(1)}, bf16[128,1024]{1,0:T(8,128)(2,1)S(1)}, u32[]{:S(2)}, u32[]{:S(2)}) %collective-permute-start.5) | collective-permute-done | bytes 262176 | tf_op jit(solution)/shard_map/ppermute | solution.py:76
  57.4 2.3 %scatter_fusion = bf16[2,12288,128]{2,1,0:T(8,128)(2,1)} fusion(bf16[2,12288,128]{2,1,0:T(8,128)(2,1)} %copy.178, s32[16]{0:T(128)S(1)} %get-tuple-element.30, bf16[16,2,128]{2,0,1:T(8,128)(2,1)S(1)} %maximum_bitcast_fusion), kind=kCustom, calls=%fused_computation.2 | custom fusion | bytes 24640 | tf_op jit(solution)/shard_map/scatter | solution.py:56
  59.8 3.4 %fusion.100 = (f32[16,5]{0,1:T(8,128)S(1)}, f32[16,5,12288]{2,0,1:T(8,128)S(1)}) fusion(bf16[2,12288,128]{2,1,0:T(8,128)(2,1)} %scatter_fusion, bf16[16,5,64]{2,0,1:T(8,128)(2,1)S(1)} %get-tuple-element.41, bf16[16,5,64]{2,0,1:T(8,128)(2,1)S(1)} %get-tuple-element.40, pred[16,12288]{1,0:T(8,128)(4,1)S(1)} %fusion.43), kind=kOutput, calls=%fused_computation.195 | convolution fusion | flops 254648240 | bytes 7295296 | tf_op jit(solution)/shard_map/ngd,md->ngm/dot_general | solution.py:32
  64.8 2.3 %collective-permute-start.7 = (bf16[16,640]{1,0:T(8,128)(2,1)S(1)}, bf16[16,640]{1,0:T(8,128)(2,1)S(1)}, u32[]{:S(2)}, u32[]{:S(2)}) collective-permute-start(bf16[16,640]{1,0:T(8,128)(2,1)S(1)} %bitcast.110), channel_id=1, source_target_pairs={{0,1},{1,0},{2,3},{3,2},{4,5},{5,4},{6,7},{7,6},{8,9},{9,8},{10,11... | collective-permute-start | bytes 61448 | tf_op jit(solution)/shard_map/ppermute | solution.py:76
  68.4 3.3 %collective-permute-start.9 = (bf16[32,640]{1,0:T(8,128)(2,1)S(1)}, bf16[32,640]{1,0:T(8,128)(2,1)S(1)}, u32[]{:S(2)}, u32[]{:S(2)}) collective-permute-start(bf16[32,640]{1,0:T(8,128)(2,1)S(1)} %get-tuple-element.62), channel_id=1, source_target_pairs={{0,4},{1,5},{2,6},{3,7},{4,0},{5,1},{6,2},{7,3},{8,12},{9,13},{10,... | collective-permute-start | bytes 122888 | tf_op jit(solution)/shard_map/ppermute | solution.py:76
  75.8 2.1 %collective-permute-start.12 = (bf16[128,640]{1,0:T(8,128)(2,1)S(1)}, bf16[128,640]{1,0:T(8,128)(2,1)S(1)}, u32[]{:S(2)}, u32[]{:S(2)}) collective-permute-start(bf16[128,640]{1,0:T(8,128)(2,1)S(1)} %get-tuple-element.50), channel_id=1, source_target_pairs={{0,16},{1,17},{2,18},{3,19},{4,20},{5,21},{6,22},{7,23},{8,24},{9,... | collective-permute-start | bytes 491528 | tf_op jit(solution)/shard_map/ppermute | solution.py:76
  77.9 2.8 %maximum_select_fusion = bf16[2,2048,128]{2,1,0:T(8,128)(2,1)} fusion(bf16[2,1024,128]{2,1,0:T(8,128)(2,1)} %collective-permute-done.14, bf16[2,1024,128]{2,1,0:T(8,128)(2,1)} %param.20, pred[]{:T(512)S(6)} %eq.32), kind=kLoop, calls=%fused_computation.38 | loop fusion | flops 4718592 | bytes 2097153 | tf_op jit(solution)/shard_map/jit(_where)/select_n | solution.py:154
  81.8 1.8 %collective-permute-done.12 = bf16[128,640]{1,0:T(8,128)(2,1)S(1)} collective-permute-done((bf16[128,640]{1,0:T(8,128)(2,1)S(1)}, bf16[128,640]{1,0:T(8,128)(2,1)S(1)}, u32[]{:S(2)}, u32[]{:S(2)}) %collective-permute-start.12) | collective-permute-done | bytes 163872 | tf_op jit(solution)/shard_map/ppermute | solution.py:76
  86.6 4.5 %copy.98 = bf16[256,4,1280]{0,2,1:T(8,128)(2,1)} copy(bf16[256,4,1280]{2,0,1:T(8,128)(2,1)} %all-to-all-done.1) | data formatting | bytes 5242880 | tf_op jit(solution)/shard_map/all_to_all | solution.py:91
  91.2 3.8 %fusion.18 = f32[256,256]{0,1:T(8,128)S(1)} fusion(bf16[256,5120]{0,1:T(8,128)(2,1)} %bitcast.95, bf16[640,8,2,128]{3,2,1,0:T(2,128)(2,1)} %bitcast.98, f32[256]{0:T(256)S(1)} %bitcast.113), kind=kOutput, calls=%fused_computation.30 | convolution fusion | flops 671154176 | bytes 5506048 | tf_op jit(solution)/shard_map/dot_general | solution.py:93
  95.7 2.3 %convolution_add_fusion = f32[256,640]{1,0:T(8,128)S(1)} fusion(bf16[256,5120]{0,1:T(8,128)(2,1)S(1)} %bitcast.96, bf16[5120,640]{1,0:T(8,128)(2,1)S(1)} %bitcast.92, f32[640]{0:T(1024)S(1)} %copy-done.8), kind=kOutput, calls=%fused_computation.29 | convolution fusion | flops 1677885440 | bytes 9832960 | tf_op jit(solution)/shard_map/dot_general | solution.py:92
  99.0 3.4 %collective-permute-start.15 = (bf16[2,256,128]{2,1,0:T(8,128)(2,1)S(1)}, bf16[2,256,128]{2,1,0:T(8,128)(2,1)}, u32[]{:S(2)}, u32[]{:S(2)}) collective-permute-start(bf16[2,256,128]{2,1,0:T(8,128)(2,1)S(1)} %pad_maximum_fusion.3), channel_id=1, source_target_pairs={{0,1},{1,0},{2,3},{3,2},{4,5},{5,4},{6,7},{7,6},{8,9},{9,8},{10,11... | collective-permute-start | bytes 393224 | tf_op jit(solution)/shard_map/ppermute | solution.py:11
  104.7 7.2 %fusion.1 = (f32[256,5]{0,1:T(8,128)S(1)}, f32[256,5,2560]{2,0,1:T(8,128)}) fusion(pred[256,2560]{1,0:T(8,128)(4,1)S(1)} %copy-done.2, bf16[2,2048,128]{2,1,0:T(8,128)(2,1)} %maximum_select_fusion, bf16[2,512,128]{2,1,0:T(8,128)(2,1)S(1)} %maximum_select_fusion.1, bf16[256,5,64]{2,0,1:T(8,128)(2,1)S(1)} %get-tuple-element.33, ...), kind=kOutput, calls=%fused_computation.7 | convolution fusion | flops 850656000 | bytes 15406080 | tf_op jit(solution)/shard_map/ngd,md->ngm/dot_general | solution.py:32
  111.9 8.5 %fusion.2 = f32[256,5]{0,1:T(8,128)S(1)} fusion(f32[256,5,2560]{2,0,1:T(8,128)} %get-tuple-element.80, f32[256,5]{0,1:T(8,128)S(1)} %get-tuple-element.79, pred[256,2560]{1,0:T(8,128)(4,1)S(1)} %copy-done.2), kind=kLoop, calls=%fused_computation.8 | loop fusion | flops 13105920 | bytes 13772800 | tf_op jit(solution)/shard_map/reduce_sum | solution.py:39
  120.4 7.0 %fusion.40 = bf16[256,5,128]{0,2,1:T(8,128)(2,1)S(1)} fusion(f32[256,5,2560]{2,0,1:T(8,128)} %get-tuple-element.80, f32[256,5]{0,1:T(8,128)S(1)} %get-tuple-element.79, pred[256,2560]{1,0:T(8,128)(4,1)S(1)} %copy-done.2, bf16[2,512,128]{2,1,0:T(8,128)(2,1)S(1)} %maximum_select_fusion.1, bf16[2,2048,128]{2,1,0:T(8,128)(2,1)S(1)} %copy-done.3, ...), kind=kOutput, calls=%fused_computation.40 | convolution fusion | flops 853606400 | bytes 15411200 | tf_op jit(solution)/shard_map/ngm,md->ngd/dot_general | solution.py:41
  (144 shorter events, 32.6 us)
Async XLA Ops:
  0.6 12.8 %copy-start.12 = (s32[16]{0:T(128)S(1)}, s32[16]{0:T(128)}, u32[]{:S(2)}) copy-start(s32[16]{0:T(128)} %param.21) | copy-start | bytes 196
  0.7 15.4 %copy-start.4 = (bf16[256,1280]{1,0:T(8,128)(2,1)S(1)}, bf16[256,1280]{1,0:T(8,128)(2,1)}, u32[]{:S(2)}) copy-start(bf16[256,1280]{1,0:T(8,128)(2,1)} %param.12) | copy-start | bytes 1966084
  7.2 70.8 %collective-permute-start.14 = (bf16[2,1024,128]{2,1,0:T(8,128)(2,1)}, bf16[2,1024,128]{2,1,0:T(8,128)(2,1)}, u32[]{:S(2)}, u32[]{:S(2)}) collective-permute-start(bf16[2,1024,128]{2,1,0:T(8,128)(2,1)} %param.20), channel_id=1, source_target_pairs={{0,1},{1,0},{2,3},{3,2},{4,5},{5,4},{6,7},{7,6},{8,9},{9,8},{10,11... | collective-permute-start | bytes 1572872 | tf_op jit(solution)/shard_map/ppermute | solution.py:11
  9.2 13.4 %all-to-all-start = ((bf16[16,4,1280]{2,0,1:T(8,128)(2,1)}), bf16[16,4,1280]{2,0,1:T(8,128)(2,1)S(1)}, u32[]{:S(2)}, u32[]{:S(2)}) async-start(bf16[16,4,1280]{2,0,1:T(8,128)(2,1)} %bitcast.88), calls=%async_computation | async-start | bytes 327680 | tf_op jit(solution)/shard_map/all_to_all | solution.py:91
  19.4 8.0 %copy-start.9 = (f32[2,128]{1,0:T(2,128)S(1)}, f32[2,128]{1,0:T(2,128)}, u32[]{:S(2)}) copy-start(f32[2,128]{1,0:T(2,128)} %param.16) | copy-start | bytes 3076
  22.7 63.9 %all-to-all-start.1 = ((bf16[256,4,1280]{2,0,1:T(8,128)(2,1)}), bf16[256,4,1280]{2,0,1:T(8,128)(2,1)}, u32[]{:S(2)}, u32[]{:S(2)}) async-start(bf16[256,4,1280]{2,0,1:T(8,128)(2,1)} %copy.97), calls=%async_computation.1 | async-start | bytes 5242880 | tf_op jit(solution)/shard_map/all_to_all | solution.py:91
  31.8 1.4 %collective-permute-start = (bf16[16,1024]{1,0:T(8,128)(2,1)S(1)}, bf16[16,1024]{1,0:T(8,128)(2,1)S(1)}, u32[]{:S(2)}, u32[]{:S(2)}) collective-permute-start(bf16[16,1024]{1,0:T(8,128)(2,1)S(1)} %concatenate.90), channel_id=1, source_target_pairs={{0,1},{1,0},{2,3},{3,2},{4,5},{5,4},{6,7},{7,6},{8,9},{9,8},{10,11... | collective-permute-start | bytes 98312 | tf_op jit(solution)/shard_map/ppermute | solution.py:76
  33.2 5.0 %collective-permute-start.1 = (bf16[32,1024]{1,0:T(8,128)(2,1)S(1)}, bf16[32,1024]{1,0:T(8,128)(2,1)S(1)}, u32[]{:S(2)}, u32[]{:S(2)}) collective-permute-start(bf16[32,1024]{1,0:T(8,128)(2,1)S(1)} %pad_maximum_fusion.4), channel_id=1, source_target_pairs={{0,2},{1,3},{2,4},{3,5},{4,6},{5,7},{6,0},{7,1},{8,10},{9,11},{10,... | collective-permute-start | bytes 196616 | tf_op jit(solution)/shard_map/ppermute | solution.py:76
  34.5 5.6 %collective-permute-start.2 = (bf16[32,1024]{1,0:T(8,128)(2,1)S(1)}, bf16[32,1024]{1,0:T(8,128)(2,1)S(1)}, u32[]{:S(2)}, u32[]{:S(2)}) collective-permute-start(bf16[32,1024]{1,0:T(8,128)(2,1)S(1)} %pad_maximum_fusion.4), channel_id=1, source_target_pairs={{0,4},{1,5},{2,6},{3,7},{4,0},{5,1},{6,2},{7,3},{8,12},{9,13},{10,... | collective-permute-start | bytes 196616 | tf_op jit(solution)/shard_map/ppermute | solution.py:76
  37.1 3.5 %collective-permute-start.3 = (bf16[32,1024]{1,0:T(8,128)(2,1)S(1)}, bf16[32,1024]{1,0:T(8,128)(2,1)S(1)}, u32[]{:S(2)}, u32[]{:S(2)}) collective-permute-start(bf16[32,1024]{1,0:T(8,128)(2,1)S(1)} %pad_maximum_fusion.4), channel_id=1, source_target_pairs={{0,6},{1,7},{2,0},{3,1},{4,2},{5,3},{6,4},{7,5},{8,14},{9,15},{10,... | collective-permute-start | bytes 196616 | tf_op jit(solution)/shard_map/ppermute | solution.py:76
  40.6 9.0 %collective-permute-start.4 = (bf16[128,1024]{1,0:T(8,128)(2,1)S(1)}, bf16[128,1024]{1,0:T(8,128)(2,1)S(1)}, u32[]{:S(2)}, u32[]{:S(2)}) collective-permute-start(bf16[128,1024]{1,0:T(8,128)(2,1)S(1)} %get-tuple-element.44), channel_id=1, source_target_pairs={{0,8},{1,9},{2,10},{3,11},{4,12},{5,13},{6,14},{7,15},{8,16},{9,17... | collective-permute-start | bytes 786440 | tf_op jit(solution)/shard_map/ppermute | solution.py:76
  42.4 13.6 %collective-permute-start.5 = (bf16[128,1024]{1,0:T(8,128)(2,1)S(1)}, bf16[128,1024]{1,0:T(8,128)(2,1)S(1)}, u32[]{:S(2)}, u32[]{:S(2)}) collective-permute-start(bf16[128,1024]{1,0:T(8,128)(2,1)S(1)} %get-tuple-element.44), channel_id=1, source_target_pairs={{0,16},{1,17},{2,18},{3,19},{4,20},{5,21},{6,22},{7,23},{8,24},{9,... | collective-permute-start | bytes 786440 | tf_op jit(solution)/shard_map/ppermute | solution.py:76
  45.8 10.4 %collective-permute-start.6 = (bf16[128,1024]{1,0:T(8,128)(2,1)S(1)}, bf16[128,1024]{1,0:T(8,128)(2,1)S(1)}, u32[]{:S(2)}, u32[]{:S(2)}) collective-permute-start(bf16[128,1024]{1,0:T(8,128)(2,1)S(1)} %get-tuple-element.44), channel_id=1, source_target_pairs={{0,24},{1,25},{2,26},{3,27},{4,28},{5,29},{6,30},{7,31},{8,0},{9,1... | collective-permute-start | bytes 786440 | tf_op jit(solution)/shard_map/ppermute | solution.py:76
  64.8 3.3 %collective-permute-start.7 = (bf16[16,640]{1,0:T(8,128)(2,1)S(1)}, bf16[16,640]{1,0:T(8,128)(2,1)S(1)}, u32[]{:S(2)}, u32[]{:S(2)}) collective-permute-start(bf16[16,640]{1,0:T(8,128)(2,1)S(1)} %bitcast.110), channel_id=1, source_target_pairs={{0,1},{1,0},{2,3},{3,2},{4,5},{5,4},{6,7},{7,6},{8,9},{9,8},{10,11... | collective-permute-start | bytes 61448 | tf_op jit(solution)/shard_map/ppermute | solution.py:76
  68.2 4.1 %collective-permute-start.8 = (bf16[32,640]{1,0:T(8,128)(2,1)S(1)}, bf16[32,640]{1,0:T(8,128)(2,1)S(1)}, u32[]{:S(2)}, u32[]{:S(2)}) collective-permute-start(bf16[32,640]{1,0:T(8,128)(2,1)S(1)} %get-tuple-element.62), channel_id=1, source_target_pairs={{0,2},{1,3},{2,4},{3,5},{4,6},{5,7},{6,0},{7,1},{8,10},{9,11},{10,... | collective-permute-start | bytes 122888 | tf_op jit(solution)/shard_map/ppermute | solution.py:76
  68.4 5.3 %collective-permute-start.9 = (bf16[32,640]{1,0:T(8,128)(2,1)S(1)}, bf16[32,640]{1,0:T(8,128)(2,1)S(1)}, u32[]{:S(2)}, u32[]{:S(2)}) collective-permute-start(bf16[32,640]{1,0:T(8,128)(2,1)S(1)} %get-tuple-element.62), channel_id=1, source_target_pairs={{0,4},{1,5},{2,6},{3,7},{4,0},{5,1},{6,2},{7,3},{8,12},{9,13},{10,... | collective-permute-start | bytes 122888 | tf_op jit(solution)/shard_map/ppermute | solution.py:76
  71.7 3.0 %collective-permute-start.10 = (bf16[32,640]{1,0:T(8,128)(2,1)S(1)}, bf16[32,640]{1,0:T(8,128)(2,1)S(1)}, u32[]{:S(2)}, u32[]{:S(2)}) collective-permute-start(bf16[32,640]{1,0:T(8,128)(2,1)S(1)} %get-tuple-element.62), channel_id=1, source_target_pairs={{0,6},{1,7},{2,0},{3,1},{4,2},{5,3},{6,4},{7,5},{8,14},{9,15},{10,... | collective-permute-start | bytes 122888 | tf_op jit(solution)/shard_map/ppermute | solution.py:76
  74.7 7.1 %collective-permute-start.11 = (bf16[128,640]{1,0:T(8,128)(2,1)S(1)}, bf16[128,640]{1,0:T(8,128)(2,1)S(1)}, u32[]{:S(2)}, u32[]{:S(2)}) collective-permute-start(bf16[128,640]{1,0:T(8,128)(2,1)S(1)} %get-tuple-element.50), channel_id=1, source_target_pairs={{0,8},{1,9},{2,10},{3,11},{4,12},{5,13},{6,14},{7,15},{8,16},{9,17... | collective-permute-start | bytes 491528 | tf_op jit(solution)/shard_map/ppermute | solution.py:76
  75.8 7.8 %collective-permute-start.12 = (bf16[128,640]{1,0:T(8,128)(2,1)S(1)}, bf16[128,640]{1,0:T(8,128)(2,1)S(1)}, u32[]{:S(2)}, u32[]{:S(2)}) collective-permute-start(bf16[128,640]{1,0:T(8,128)(2,1)S(1)} %get-tuple-element.50), channel_id=1, source_target_pairs={{0,16},{1,17},{2,18},{3,19},{4,20},{5,21},{6,22},{7,23},{8,24},{9,... | collective-permute-start | bytes 491528 | tf_op jit(solution)/shard_map/ppermute | solution.py:76
  80.8 4.5 %collective-permute-start.13 = (bf16[128,640]{1,0:T(8,128)(2,1)S(1)}, bf16[128,640]{1,0:T(8,128)(2,1)S(1)}, u32[]{:S(2)}, u32[]{:S(2)}) collective-permute-start(bf16[128,640]{1,0:T(8,128)(2,1)S(1)} %get-tuple-element.50), channel_id=1, source_target_pairs={{0,24},{1,25},{2,26},{3,27},{4,28},{5,29},{6,30},{7,31},{8,0},{9,1... | collective-permute-start | bytes 491528 | tf_op jit(solution)/shard_map/ppermute | solution.py:76
  86.6 8.4 %slice-start = ((s8[6553600]{0:T(1024)(128)(4,1)}), s8[2359296]{0:T(1024)(128)(4,1)S(1)}, s32[]{:S(2)}) async-start(s8[6553600]{0:T(1024)(128)(4,1)} %bitcast.91), calls=%async_computation.2 | async-start | bytes 4718592
  99.0 12.9 %copy-start.6 = (bf16[2,256,128]{2,1,0:T(8,128)(2,1)}, bf16[2,256,128]{2,1,0:T(8,128)(2,1)S(1)}, u32[]{:S(2)}) copy-start(bf16[2,256,128]{2,1,0:T(8,128)(2,1)S(1)} %pad_maximum_fusion.3) | copy-start | bytes 393220
  99.0 4.5 %collective-permute-start.15 = (bf16[2,256,128]{2,1,0:T(8,128)(2,1)S(1)}, bf16[2,256,128]{2,1,0:T(8,128)(2,1)}, u32[]{:S(2)}, u32[]{:S(2)}) collective-permute-start(bf16[2,256,128]{2,1,0:T(8,128)(2,1)S(1)} %pad_maximum_fusion.3), channel_id=1, source_target_pairs={{0,1},{1,0},{2,3},{3,2},{4,5},{5,4},{6,7},{7,6},{8,9},{9,8},{10,11... | collective-permute-start | bytes 393224 | tf_op jit(solution)/shard_map/ppermute | solution.py:11
  111.9 8.5 %copy-start.3 = (bf16[2,2048,128]{2,1,0:T(8,128)(2,1)S(1)}, bf16[2,2048,128]{2,1,0:T(8,128)(2,1)}, u32[]{:S(2)}) copy-start(bf16[2,2048,128]{2,1,0:T(8,128)(2,1)} %maximum_select_fusion) | copy-start | bytes 3145732
  (11 other events, 55.5 us)
